TPU v7x, 256 devices: a whole 4x4x8 slice. The times are simulated.
256 devices in a mesh: section: 2 (over core), seq: 16 (over x, y), exp: 8 (over z).
Axes of the slice: x: 4, y: 4, z: 8, core: 2. Of those that a mesh axis runs over, the one named last changes fastest.
Arguments:
- hidden_in: bfloat16 [2048, 2048], P('seq'), may hold values from -6 to 6
- seg_ids: int32 [2048], P('seq'), may hold values from 0 to 7, never falling along the last dimension, each value on 1 to 1024 neighbouring positions
- attn_gain: float32 [2048], replicated, may hold values from 0.25 to 1.75
- w_query: bfloat16 [2048, 2048], P(None, ('section', 'exp'))
- w_key: bfloat16 [2048, 2048], P(None, ('section', 'exp'))
- w_value: bfloat16 [2048, 2048], P(None, ('section', 'exp')), may hold values from -0.125 to 0.125
- w_out: bfloat16 [2048, 2048], P(('section', 'exp')), may hold values from -0.5 to 0.5
- moe_gain: float32 [2048], replicated, may hold values from 0.25 to 1.75
- expert_ids: int32 [2048, 8], P(('seq', 'exp')), may hold values from 0 to 63, all different within a row; in each aligned block of 16 rows (0 to 15, 16 to 31, ...) at most 4 rows name the same one
- route_weights: float32 [2048, 8], P(('seq', 'exp')), may hold values from 0.1 to 0.6
- gate_halves: bfloat16 [128, 2048, 512], P(('seq', 'exp'), None, 'section'), may hold values from -0.125 to 0.125
- up_halves: bfloat16 [128, 2048, 512], P(('seq', 'exp'), None, 'section'), may hold values from -0.125 to 0.125
- down_halves: bfloat16 [128, 512, 2048], P(('seq', 'exp'), 'section'), may hold values from -0.1875 to 0.1875
Outputs:
- layer_out: bfloat16 [2048, 2048], P(('seq', 'exp'))
Inputs may be any that keep to these rules, and one draw needn't show every extreme that they name: `seg_ids`: prompt numbers never fall along the batch; each prompt holds 1 to 1024 tokens, and one holds exactly 1024. `expert_ids`: A token's 8 experts are distinct. In each aligned block of 16 tokens (the tokens of one device along seq and exp), no expert is chosen by more than 4 of the block's tokens, a bound that some block reaches.
All inputs are finite; a program needn't handle non-finite values.
Results may differ from a plain program's by a relative error of at most 0.012.
Values may be sent and summed in bfloat16 or wider, within the bound.
No kernel may reach another device: no remote copies, remote signals or barrier semaphores. Data moves between devices by JAX's collectives and lax.ppermute only.
A program may use at most 64 MiB of HBM per device.

v0:
```python
import math
import jax
import jax.numpy as jnp
from jax import lax
from jax.sharding import PartitionSpec as P

epsilon = 1e-05
rope_base = 10000.0


def rms_scale(rows, gain):
    wide = rows.astype(jnp.float32)
    inverse = lax.rsqrt(jnp.mean(wide * wide, axis=-1, keepdims=True) + epsilon)
    return (wide * inverse * gain).astype(jnp.bfloat16)


def rotate(values, positions):
    half_dim = values.shape[-1] // 2
    frequency = rope_base ** (-2.0 * jnp.arange(half_dim, dtype=jnp.float32) / values.shape[-1])
    angles = positions.astype(jnp.float32)[:, None] * frequency[None, :]
    cosine = jnp.cos(angles)
    sine_part = jnp.sin(angles)
    first_half = values[:, :half_dim]
    second_half = values[:, half_dim:]
    return jnp.concatenate(
        [
            first_half * cosine - second_half * sine_part,
            second_half * cosine + first_half * sine_part,
        ],
        axis=-1,
    )


def per_device(
    hidden_in,
    seg_ids,
    attn_gain,
    w_query,
    w_key,
    w_value,
    w_out,
    moe_gain,
    expert_ids,
    route_weights,
    gate_halves,
    up_halves,
    down_halves,
):
    tok_seq = hidden_in.shape[0]
    width = hidden_in.shape[1]
    head_dim = w_query.shape[1]
    positions = lax.axis_index("seq") * tok_seq + jnp.arange(tok_seq, dtype=jnp.int32)
    normed = rms_scale(hidden_in, attn_gain)
    query_rows = rotate(
        jnp.dot(normed, w_query, preferred_element_type=jnp.float32), positions
    ).astype(jnp.bfloat16)
    key_rows = rotate(jnp.dot(normed, w_key, preferred_element_type=jnp.float32), positions).astype(
        jnp.bfloat16
    )
    value_rows = jnp.dot(normed, w_value, preferred_element_type=jnp.float32).astype(jnp.bfloat16)
    score_scale = 1.0 / math.sqrt(head_dim)
    run_max = jnp.full((tok_seq,), -1e30, jnp.float32)
    piece_keys = lax.all_gather(key_rows, "seq", axis=0, tiled=True)
    piece_values = lax.all_gather(value_rows, "seq", axis=0, tiled=True)
    key_segs = lax.all_gather(seg_ids, "seq", axis=0, tiled=True)
    piece_rows = piece_keys.shape[0]
    scores = (
        lax.dot_general(
            query_rows, piece_keys, (((1,), (1,)), ((), ())), preferred_element_type=jnp.float32
        )
        * score_scale
    )
    key_pos = jnp.arange(piece_rows, dtype=jnp.int32)
    allowed = (seg_ids[:, None] == key_segs[None, :]) & (key_pos[None, :] <= positions[:, None])
    masked = jnp.where(allowed, scores, -1e30)
    new_max = jnp.maximum(run_max, jnp.max(masked, axis=1))
    weights = jnp.where(allowed, jnp.exp(masked - new_max[:, None]), 0.0)
    run_total = jnp.sum(weights, axis=1)
    weighted_sum = jnp.dot(
        weights.astype(jnp.bfloat16), piece_values, preferred_element_type=jnp.float32
    )
    run_max, run_total, weighted_sum = (new_max, run_total, weighted_sum)
    head_out = (weighted_sum / run_total[:, None]).astype(jnp.bfloat16)
    partial_value = jnp.dot(head_out, w_out, preferred_element_type=jnp.float32)
    tok_dev = tok_seq // lax.axis_size("exp")
    own_start = lax.axis_index("exp") * tok_dev
    summed = lax.psum(partial_value, ("section", "exp"))
    summed = lax.dynamic_slice_in_dim(summed, own_start, tok_dev, 0)
    own_rows = lax.dynamic_slice_in_dim(hidden_in, own_start, tok_dev, 0)
    residual = (own_rows.astype(jnp.float32) + summed).astype(jnp.bfloat16)
    moe_in = rms_scale(residual, moe_gain)
    experts = lax.axis_size("seq") * lax.axis_size("exp") // 2
    top_count = expert_ids.shape[1]
    capacity = min(tok_dev, max(2, 2 * tok_dev * top_count // experts))
    row_count = tok_dev * top_count
    flat_ids = expert_ids.reshape(row_count)
    one_hot = (flat_ids[:, None] == jnp.arange(experts, dtype=jnp.int32)[None, :]).astype(jnp.int32)
    slot_rank = jnp.sum((jnp.cumsum(one_hot, axis=0) - one_hot) * one_hot, axis=1)
    slot_index = flat_ids * capacity + slot_rank
    placed = slot_index[:, None] == jnp.arange(experts * capacity, dtype=jnp.int32)[None, :]
    repeated = jnp.repeat(moe_in, top_count, axis=0)
    outgoing = lax.dot_general(
        placed.astype(jnp.bfloat16),
        repeated,
        (((0,), (0,)), ((), ())),
        preferred_element_type=jnp.float32,
    ).astype(jnp.bfloat16)
    row_token = jnp.arange(row_count, dtype=jnp.int32) // top_count
    token_hot = (row_token[None, :] == jnp.arange(tok_dev, dtype=jnp.int32)[:, None]).astype(
        jnp.float32
    )
    weighted = token_hot * route_weights.reshape(row_count)[None, :]
    combine = jnp.dot(weighted, placed.astype(jnp.float32), precision=lax.Precision.HIGHEST)
    doubled = jnp.broadcast_to(
        outgoing.reshape(experts, 1, capacity, width), (experts, 2, capacity, width)
    ).reshape(2 * experts, capacity, width)
    arrived = lax.all_to_all(doubled, ("seq", "exp"), split_axis=0, concat_axis=0, tiled=True)
    flat_rows = arrived.reshape(-1, width)
    gate_proj = jnp.dot(flat_rows, gate_halves[0], preferred_element_type=jnp.float32)
    up_proj = jnp.dot(flat_rows, up_halves[0], preferred_element_type=jnp.float32)
    activated = (jax.nn.silu(gate_proj) * up_proj).astype(jnp.bfloat16)
    returned = lax.all_to_all(
        jnp.dot(activated, down_halves[0], preferred_element_type=jnp.float32)
        .astype(jnp.bfloat16)
        .reshape(arrived.shape),
        ("seq", "exp"),
        split_axis=0,
        concat_axis=0,
        tiled=True,
    )
    halves_sum = jnp.sum(
        returned.reshape(experts, 2, capacity, width).astype(jnp.float32), axis=1
    ).reshape(experts * capacity, width)
    moe_part = jnp.dot(combine, halves_sum, precision=lax.Precision.HIGHEST)
    moe_total = lax.psum(moe_part, "section")
    return (residual.astype(jnp.float32) + moe_total).astype(jnp.bfloat16)


def solution(mesh):
    in_specs = (
        P("seq", None),
        P("seq"),
        P(),
        P(None, ("section", "exp")),
        P(None, ("section", "exp")),
        P(None, ("section", "exp")),
        P(("section", "exp"), None),
        P(),
        P(("seq", "exp"), None),
        P(("seq", "exp"), None),
        P(("seq", "exp"), None, "section"),
        P(("seq", "exp"), None, "section"),
        P(("seq", "exp"), "section", None),
    )
    out_specs = P(("seq", "exp"), None)
    return jax.shard_map(
        per_device, mesh=mesh, in_specs=in_specs, out_specs=out_specs, check_vma=False
    )
```

profile of v0, /device:TPU:1, one launch (start us, length us, event | category | flops | bytes accessed | tf_op | source)
XLA Modules:
  0.0 376.0 jit_solution(10940934380651629049)
XLA Ops:
  6.5 0.0 copy-start
  6.5 0.0 copy-start.4
  6.5 0.0 all-reduce.3.cloned.1.call-start
  6.6 1.3 fusion.4
  7.9 1.6 fusion.74
  9.5 0.0 copy-start.2
  9.5 0.0 copy-start.7
  9.6 0.0 copy-start.8
  9.6 1.7 fusion.76
  11.3 0.2 fusion.52
  11.5 20.5 %all_gather.10 = bf16[2048,128]{0,1:T(8,128)(2,1)S(1)} all-gather(bf16[128,128]{0,1:T(8,128)(2,1)S(1)} %pad_maximum_fusion), channel_id=1, replica_groups=mesh['section'=2,'seq'=16,'exp'=8] {'seq'}, dimensions={0}, use_global_device_ids=true | all-gather | bytes 557056 | tf_op jit(solution)/shard_map/all_gather | solution.py:63
  32.0 0.0 copy-done.4
  32.0 15.7 %all-gather = s32[16,1,128]{2,1,0:T(1,128)S(1)} all-gather(s32[1,1,128]{2,1,0:T(1,128)S(1)} %bitcast.33), channel_id=1, replica_groups=mesh['section'=2,'seq'=16,'exp'=8] {'seq'}, dimensions={0}, use_global_device_ids=true | all-gather | bytes 8704 | tf_op jit(solution)/shard_map/all_gather | solution.py:65
  47.8 0.5 fusion.78
  48.3 0.0 copy-done.2
  48.3 0.0 copy-done.7
  48.3 0.0 copy-done.8
  48.3 0.4 convolution_convert_fusion.2
  48.7 16.1 %all_gather.11 = bf16[2048,128]{1,0:T(8,128)(2,1)S(1)} all-gather(bf16[128,128]{1,0:T(8,128)(2,1)S(1)} %convolution_convert_fusion.2), channel_id=1, replica_groups=mesh['section'=2,'seq'=16,'exp'=8] {'seq'}, dimensions={0}, use_global_device_ids=true | all-gather | bytes 557056 | tf_op jit(solution)/shard_map/all_gather | solution.py:64
  64.8 0.4 fusion.13
  65.2 0.0 copy-start.5
  65.2 0.0 copy-start.3
  65.2 2.8 fusion.3
  68.0 0.0 all-reduce.3.cloned.1.call-update
  68.1 0.0 copy-done.5
  68.1 0.1 copy.19
  68.1 0.1 reshape.82
  68.2 0.1 fusion.42
  68.3 0.2 reduce_window_sum.11
  68.5 0.2 select_reduce_fusion
  68.7 128.0 %all-reduce.3.cloned.1.call-done = f32[128,2048]{1,0:T(8,128)} async-done(((f32[128,2048]{1,0:T(8,128)}), f32[128,2048]{1,0:T(8,128)}) %all-reduce.3.cloned.1.call-update) | async-done | bytes 1048592 | tf_op jit(solution)/shard_map/psum | solution.py:87
  196.7 1.0 fusion.35
  197.7 0.0 copy-done.3
  197.7 0.1 fusion.37
  197.8 0.5 convolution_convert_fusion.1
  198.4 0.4 broadcast_in_dim.19
  198.8 1.2 broadcast_in_dim.20
  200.1 63.0 %all_to_all.10 = bf16[128,4,2048]{2,1,0:T(4,128)(2,1)S(1)} all-to-all(bf16[128,4,2048]{2,1,0:T(4,128)(2,1)S(1)} %bitcast.29), channel_id=1, replica_groups=mesh['section'=2,'seq'=16,'exp'=8] {'seq','exp'}, dimensions={0} | all-to-all | bytes 4194304 | tf_op jit(solution)/shard_map/all_to_all | solution.py:117
  263.1 2.1 reshape.85
  265.1 0.0 copy-start.1
  265.1 3.5 fusion.10
  268.7 0.0 copy-done
  268.7 0.0 copy-done.1
  268.7 5.0 %convolution_convert_fusion = bf16[512,2048]{1,0:T(8,128)(2,1)} fusion(bf16[512,2048]{1,0:T(8,128)(2,1)S(1)} %copy-done.1, bf16[1,256,2048]{2,1,0:T(8,128)(2,1)S(1)} %copy-done, bf16[1,2048,256]{2,1,0:T(8,128)(2,1)} %param.24, f32[512,256]{1,0:T(8,128)} %fusion.10), kind=kOutput, calls=%fused_computation.1 | convolution fusion | flops 1075576832 | bytes 6815744 | tf_op jit(solution)/shard_map/dot_general | solution.py:123
  273.7 4.1 %reshape.86 = bf16[128,4,2048]{2,1,0:T(4,128)(2,1)} reshape(bf16[512,2048]{1,0:T(8,128)(2,1)} %convolution_convert_fusion) | data formatting | bytes 4194304 | tf_op jit(solution)/shard_map/reshape | solution.py:125
  277.8 0.0 copy-start.6
  277.8 6.7 %all-to-all-start.1 = ((bf16[128,4,2048]{2,1,0:T(4,128)(2,1)}), bf16[128,4,2048]{2,1,0:T(4,128)(2,1)S(1)}, u32[]{:S(2)}, u32[]{:S(2)}) async-start(bf16[128,4,2048]{2,1,0:T(4,128)(2,1)} %reshape.86), calls=%async_computation.1 | async-start | bytes 4194304 | tf_op jit(solution)/shard_map/all_to_all | solution.py:122
  284.6 0.2 all-reduce.5.cloned.1.call-start
  284.8 0.0 copy-done.6
  284.8 0.1 copy.18
  284.9 0.1 mul.147
  285.0 0.2 fusion.39
  285.2 49.4 %all-to-all-done.1 = bf16[128,4,2048]{2,1,0:T(4,128)(2,1)S(1)} async-done(((bf16[128,4,2048]{2,1,0:T(4,128)(2,1)}), bf16[128,4,2048]{2,1,0:T(4,128)(2,1)S(1)}, u32[]{:S(2)}, u32[]{:S(2)}) %all-to-all-start.1) | async-done | bytes 2097184 | tf_op jit(solution)/shard_map/all_to_all | solution.py:122
  334.5 2.7 convert_reduce_fusion
  337.2 2.0 reshape.87
  339.2 1.8 fusion.79
  341.0 0.0 all-reduce.5.cloned.1.call-update
  341.0 26.6 %all-reduce.5.cloned.1.call-done = f32[16,2048]{1,0:T(8,128)} async-done(((f32[16,2048]{1,0:T(8,128)}), f32[16,2048]{1,0:T(8,128)}) %all-reduce.5.cloned.1.call-update) | async-done | bytes 131088 | tf_op jit(solution)/shard_map/psum | solution.py:135
  367.6 1.5 fusion.38
  (9 shorter events, 0.1 us)
Async XLA Ops:
  6.5 262.1 %copy-start = (bf16[1,256,2048]{2,1,0:T(8,128)(2,1)S(1)}, bf16[1,256,2048]{2,1,0:T(8,128)(2,1)}, u32[]{:S(2)}) copy-start(bf16[1,256,2048]{2,1,0:T(8,128)(2,1)} %param.25) | copy-start | bytes 3145732
  6.5 25.5 %copy-start.4 = (s32[128]{0:T(128)S(1)}, s32[128]{0:T(128)}, u32[]{:S(2)}) copy-start(s32[128]{0:T(128)} %param.14) | copy-start | bytes 1540
  6.5 190.1 %all-reduce.3.cloned.1.call-start = ((), (), s32[]{:S(2)}) async-start(), calls=%async_computation.2 | async-start | bytes 2097152 | tf_op jit(solution)/shard_map/psum | solution.py:87
  9.5 38.8 %copy-start.2 = (bf16[128,2048]{1,0:T(8,128)(2,1)S(1)}, bf16[128,2048]{1,0:T(8,128)(2,1)}, u32[]{:S(2)}) copy-start(bf16[128,2048]{1,0:T(8,128)(2,1)} %param.13) | copy-start | bytes 1572868
  9.5 38.8 %copy-start.7 = (bf16[2048,128]{1,0:T(8,128)(2,1)S(1)}, bf16[2048,128]{1,0:T(8,128)(2,1)}, u32[]{:S(2)}) copy-start(bf16[2048,128]{1,0:T(8,128)(2,1)} %param.18) | copy-start | bytes 1572868
  9.6 38.8 %copy-start.8 = (f32[2048]{0:T(1024)S(1)}, f32[2048]{0:T(1024)}, u32[]{:S(2)}) copy-start(f32[2048]{0:T(1024)} %param.15) | copy-start | bytes 24580
  65.2 2.8 copy-start.5
  65.2 132.5 %copy-start.3 = (f32[2048]{0:T(1024)S(1)}, f32[2048]{0:T(1024)}, u32[]{:S(2)}) copy-start(f32[2048]{0:T(1024)} %param.20) | copy-start | bytes 24580
  265.1 3.5 copy-start.1
  277.8 7.0 %copy-start.6 = (f32[16,8]{0,1:T(8,128)S(1)}, f32[16,8]{0,1:T(8,128)}, u32[]{:S(2)}) copy-start(f32[16,8]{0,1:T(8,128)} %param.22) | copy-start | bytes 1540
  277.8 56.7 %all-to-all-start.1 = ((bf16[128,4,2048]{2,1,0:T(4,128)(2,1)}), bf16[128,4,2048]{2,1,0:T(4,128)(2,1)S(1)}, u32[]{:S(2)}, u32[]{:S(2)}) async-start(bf16[128,4,2048]{2,1,0:T(4,128)(2,1)} %reshape.86), calls=%async_computation.1 | async-start | bytes 4194304 | tf_op jit(solution)/shard_map/all_to_all | solution.py:122
  284.6 83.1 %all-reduce.5.cloned.1.call-start = ((), (), s32[]{:S(2)}) async-start(), calls=%async_computation.3 | async-start | bytes 262144 | tf_op jit(solution)/shard_map/psum | solution.py:135
Sparse Core Ops, SparseCore 0:
  68.2 128.4 all-reduce.2
  341.1 26.4 all-reduce.4
where the time goes:
time: 377 us; the launch traced here: 376 us
  waiting for transfers between devices  204 us (54%)
  blocking collectives  115 us (31%)
  matrix products  18 us (5%)
  between operations  13.6 us (4%)
  local copies, waits for them, and re-layouts  10.2 us (3%)
  other arithmetic  7.82 us (2%)
  starting transfers between devices  6.96 us (2%)
    psum x1, waiting for transfers between devices, per_device(): summed = lax.psum(partial_value, ('section', 'exp'))  128 us
    all_to_all x1, blocking collectives, per_device(): lax.all_to_all(doubled, ('seq', 'exp'), split_axis=0, concat_axis=0, tile...  63 us
    all_to_all x1, waiting for transfers between devices, per_device(): lax.all_to_all(jnp.dot(activated, down_halves[0], preferred_element_type=...  49.4 us
    psum x1, waiting for transfers between devices, per_device(): moe_total = lax.psum(moe_part, 'section')  26.6 us
    all_gather x1, blocking collectives, per_device(): piece_keys = lax.all_gather(key_rows, 'seq', axis=0, tiled=True)  20.5 us
    all_gather x1, blocking collectives, per_device(): piece_values = lax.all_gather(value_rows, 'seq', axis=0, tiled=True)  16.1 us
    all_gather x1, blocking collectives, per_device(): key_segs = lax.all_gather(seg_ids, 'seq', axis=0, tiled=True)  15.7 us
  transfers between devices with their start and end apart: 3, of which 3 were waited for; matrix products, arithmetic and copies ran while one was open for 0% of the time, Pallas kernels for 0%

commit v1 on v0

--- a/solution.py
+++ b/solution.py
@@ -6,6 +6,12 @@
 
 epsilon = 1e-05
 rope_base = 10000.0
+
+
+def joined_along(blocks, dim):
+    shape = list(blocks.shape[1:])
+    shape[dim] *= blocks.shape[0]
+    return jnp.moveaxis(blocks, 0, dim).reshape(shape)
 
 
 def rms_scale(rows, gain):
@@ -61,7 +67,19 @@
     score_scale = 1.0 / math.sqrt(head_dim)
     run_max = jnp.full((tok_seq,), -1e30, jnp.float32)
     piece_keys = lax.all_gather(key_rows, "seq", axis=0, tiled=True)
-    piece_values = lax.all_gather(value_rows, "seq", axis=0, tiled=True)
+    size = lax.axis_size("seq")
+    pairs = [(i, (i + 1) % size) for i in range(size)]
+    back = [(b, a) for a, b in pairs]
+    lower, upper = ([], [])
+    for step in range(size - 1):
+        if step % 2 == 0:
+            lower.append(lax.ppermute(lower[-1] if lower else value_rows, "seq", pairs))
+        else:
+            upper.append(lax.ppermute(upper[-1] if upper else value_rows, "seq", back))
+    pieces = jnp.stack([*lower[::-1], value_rows, *upper])
+    shift = lax.axis_index("seq") - len(lower)
+    pieces = pieces[(jnp.arange(size) - shift) % size]
+    piece_values = joined_along(pieces, 0)
     key_segs = lax.all_gather(seg_ids, "seq", axis=0, tiled=True)
     piece_rows = piece_keys.shape[0]
     scores = (

time: 377 us -> 408 us (1.082)
  starting transfers between devices: 6.96 us -> 40.5 us
  blocking collectives: 115 us -> 98.5 us
  local copies, waits for them, and re-layouts: 10.2 us -> 21.7 us
    ppermute x0 -> x15, starting transfers between devices: none -> 33.4 us  [the longest x7 29.9 us: per_device(): upper.append(lax.ppermute(upper[-1] if upper else value_rows, 'seq', back))]
    all_gather x1 -> x0, blocking collectives: 16.1 us -> none  [per_device(): piece_values = lax.all_gather(value_rows, 'seq', axis=0, tiled=True)]
    unnamed x20 -> x35, local copies, waits for them, and re-layouts: 0.19 us -> 9.38 us
    ppermute x0 -> x15, waiting for transfers between devices: none -> 4.54 us  [the longest x7 4.51 us: per_device(): upper.append(lax.ppermute(upper[-1] if upper else value_rows, 'seq', back))]
  transfers between devices with their start and end apart: 3 -> 18, of which waited for: 3 -> 8; matrix products, arithmetic and copies ran while one was open for 0% -> 3% of each run, Pallas kernels for 0% -> 0%
where the time goes in v1:
time: 408 us; the launch traced here: 407 us
  waiting for transfers between devices  207 us (51%)
  blocking collectives  98.5 us (24%)
  starting transfers between devices  40.5 us (10%)
  local copies, waits for them, and re-layouts  21.7 us (5%)
  matrix products  17.9 us (4%)
  between operations  13.7 us (3%)
  other arithmetic  7.87 us (2%)
    psum x1, waiting for transfers between devices, per_device(): summed = lax.psum(partial_value, ('section', 'exp'))  126 us
    all_to_all x1, blocking collectives, per_device(): lax.all_to_all(doubled, ('seq', 'exp'), split_axis=0, concat_axis=0, tile...  63 us
    all_to_all x1, waiting for transfers between devices, per_device(): lax.all_to_all(jnp.dot(activated, down_halves[0], preferred_element_type=...  49.3 us
    ppermute x7, starting transfers between devices, per_device(): upper.append(lax.ppermute(upper[-1] if upper else value_rows, 'seq', back))  29.9 us
    psum x1, waiting for transfers between devices, per_device(): moe_total = lax.psum(moe_part, 'section')  26.6 us
    all_gather x1, blocking collectives, per_device(): piece_keys = lax.all_gather(key_rows, 'seq', axis=0, tiled=True)  19.6 us
    all_gather x1, blocking collectives, per_device(): key_segs = lax.all_gather(seg_ids, 'seq', axis=0, tiled=True)  15.9 us
    unnamed x35, local copies, waits for them, and re-layouts  9.38 us
  transfers between devices with their start and end apart: 18, of which 8 were waited for; matrix products, arithmetic and copies ran while one was open for 3% of the time, Pallas kernels for 0%

profile of v1, /device:TPU:1, one launch (start us, length us, event | category | flops | bytes accessed | tf_op | source)
XLA Modules:
  0.0 407.2 jit_solution(10836627285836656292)
XLA Ops:
  6.6 1.4 fusion.4
  8.0 1.6 convolution_convert_fusion.2
  9.6 2.2 collective-permute-start
  11.8 3.7 collective-permute-start.8
  15.5 1.6 fusion.76
  17.2 0.4 fusion.78
  17.6 0.2 fusion.52
  17.9 19.6 %all_gather.7 = bf16[2048,128]{0,1:T(8,128)(2,1)S(1)} all-gather(bf16[128,128]{0,1:T(8,128)(2,1)S(1)} %pad_maximum_fusion), channel_id=1, replica_groups=mesh['section'=2,'seq'=16,'exp'=8] {'seq'}, dimensions={0}, use_global_device_ids=true | all-gather | bytes 557056 | tf_op jit(solution)/shard_map/all_gather | solution.py:69
  37.5 1.2 collective-permute-start.2
  38.8 15.9 %all-gather = s32[16,1,128]{2,1,0:T(1,128)S(1)} all-gather(s32[1,1,128]{2,1,0:T(1,128)S(1)} %bitcast.69), channel_id=1, replica_groups=mesh['section'=2,'seq'=16,'exp'=8] {'seq'}, dimensions={0}, use_global_device_ids=true | all-gather | bytes 8704 | tf_op jit(solution)/shard_map/all_gather | solution.py:83
  54.7 1.5 collective-permute-start.9
  56.2 0.5 fusion.80
  56.7 1.1 collective-permute-done.9
  57.8 4.5 %collective-permute-start.10 = (bf16[128,128]{1,0:T(8,128)(2,1)S(1)}, bf16[128,128]{1,0:T(8,128)(2,1)S(1)}, u32[]{:S(2)}, u32[]{:S(2)}) collective-permute-start(bf16[128,128]{1,0:T(8,128)(2,1)S(1)} %collective-permute-done.9), channel_id=1, source_target_pairs={{8,0},{16,8},{24,16},{32,24},{40,32},{48,40},{56,48},{64,56},{72,6... | collective-permute-start | bytes 98312 | tf_op jit(solution)/shard_map/ppermute | solution.py:78
  62.3 1.0 collective-permute-done.10
  63.3 5.1 %collective-permute-start.11 = (bf16[128,128]{1,0:T(8,128)(2,1)S(1)}, bf16[128,128]{1,0:T(8,128)(2,1)S(1)}, u32[]{:S(2)}, u32[]{:S(2)}) collective-permute-start(bf16[128,128]{1,0:T(8,128)(2,1)S(1)} %collective-permute-done.10), channel_id=1, source_target_pairs={{8,0},{16,8},{24,16},{32,24},{40,32},{48,40},{56,48},{64,56},{72,6... | collective-permute-start | bytes 98312 | tf_op jit(solution)/shard_map/ppermute | solution.py:78
  68.3 0.4 fusion.13
  68.8 0.6 collective-permute-done.11
  69.4 5.1 %collective-permute-start.12 = (bf16[128,128]{1,0:T(8,128)(2,1)S(1)}, bf16[128,128]{1,0:T(8,128)(2,1)S(1)}, u32[]{:S(2)}, u32[]{:S(2)}) collective-permute-start(bf16[128,128]{1,0:T(8,128)(2,1)S(1)} %collective-permute-done.11), channel_id=1, source_target_pairs={{8,0},{16,8},{24,16},{32,24},{40,32},{48,40},{56,48},{64,56},{72,6... | collective-permute-start | bytes 98312 | tf_op jit(solution)/shard_map/ppermute | solution.py:78
  74.4 1.0 collective-permute-done.12
  75.4 5.1 %collective-permute-start.13 = (bf16[128,128]{1,0:T(8,128)(2,1)S(1)}, bf16[128,128]{1,0:T(8,128)(2,1)S(1)}, u32[]{:S(2)}, u32[]{:S(2)}) collective-permute-start(bf16[128,128]{1,0:T(8,128)(2,1)S(1)} %collective-permute-done.12), channel_id=1, source_target_pairs={{8,0},{16,8},{24,16},{32,24},{40,32},{48,40},{56,48},{64,56},{72,6... | collective-permute-start | bytes 98312 | tf_op jit(solution)/shard_map/ppermute | solution.py:78
  80.6 0.1 reshape.135
  80.7 0.8 collective-permute-done.13
  81.5 5.1 %collective-permute-start.14 = (bf16[128,128]{1,0:T(8,128)(2,1)S(1)}, bf16[128,128]{1,0:T(8,128)(2,1)S(1)}, u32[]{:S(2)}, u32[]{:S(2)}) collective-permute-start(bf16[128,128]{1,0:T(8,128)(2,1)S(1)} %collective-permute-done.13), channel_id=1, source_target_pairs={{8,0},{16,8},{24,16},{32,24},{40,32},{48,40},{56,48},{64,56},{72,6... | collective-permute-start | bytes 98312 | tf_op jit(solution)/shard_map/ppermute | solution.py:78
  86.6 0.6 constant_dynamic-update-slice_fusion.15
  87.2 0.6 constant_dynamic-update-slice_fusion.14
  87.8 0.6 constant_dynamic-update-slice_fusion.13
  88.4 0.6 constant_dynamic-update-slice_fusion.12
  89.1 0.6 constant_dynamic-update-slice_fusion.11
  89.7 0.6 constant_dynamic-update-slice_fusion.10
  90.3 0.6 constant_dynamic-update-slice_fusion.9
  90.9 0.6 constant_dynamic-update-slice_fusion.8
  91.5 0.6 constant_dynamic-update-slice_fusion.7
  92.1 0.6 constant_dynamic-update-slice_fusion.6
  92.7 0.6 constant_dynamic-update-slice_fusion.5
  93.3 0.6 constant_dynamic-update-slice_fusion.4
  94.0 0.6 constant_dynamic-update-slice_fusion.3
  94.6 0.6 constant_dynamic-update-slice_fusion.2
  95.2 0.6 constant_dynamic-update-slice_fusion.1
  95.8 0.6 constant_dynamic-update-slice_fusion
  96.4 1.7 gather_fusion
  98.1 2.8 fusion.3
  101.0 0.2 reduce_window_sum.11
  101.2 0.2 select_reduce_fusion
  101.4 126.5 %all-reduce.3.cloned.1.call-done = f32[128,2048]{1,0:T(8,128)} async-done(((f32[128,2048]{1,0:T(8,128)}), f32[128,2048]{1,0:T(8,128)}) %all-reduce.3.cloned.1.call-update) | async-done | bytes 1048592 | tf_op jit(solution)/shard_map/psum | solution.py:105
  227.9 1.0 fusion.35
  229.0 0.5 convolution_convert_fusion.1
  229.6 0.4 broadcast_in_dim.19
  230.0 1.2 broadcast_in_dim.20
  231.2 63.0 %all_to_all.10 = bf16[128,4,2048]{2,1,0:T(4,128)(2,1)S(1)} all-to-all(bf16[128,4,2048]{2,1,0:T(4,128)(2,1)S(1)} %bitcast.64), channel_id=1, replica_groups=mesh['section'=2,'seq'=16,'exp'=8] {'seq','exp'}, dimensions={0} | all-to-all | bytes 4194304 | tf_op jit(solution)/shard_map/all_to_all | solution.py:135
  294.3 2.1 reshape.138
  296.3 3.5 fusion.10
  299.9 5.0 %convolution_convert_fusion = bf16[512,2048]{1,0:T(8,128)(2,1)} fusion(bf16[512,2048]{1,0:T(8,128)(2,1)S(1)} %copy-done.1, bf16[1,256,2048]{2,1,0:T(8,128)(2,1)S(1)} %copy-done, bf16[1,2048,256]{2,1,0:T(8,128)(2,1)} %param.24, f32[512,256]{1,0:T(8,128)} %fusion.10), kind=kOutput, calls=%fused_computation.2 | convolution fusion | flops 1075576832 | bytes 6815744 | tf_op jit(solution)/shard_map/dot_general | solution.py:141
  304.9 4.1 %reshape.139 = bf16[128,4,2048]{2,1,0:T(4,128)(2,1)} reshape(bf16[512,2048]{1,0:T(8,128)(2,1)} %convolution_convert_fusion) | data formatting | bytes 4194304 | tf_op jit(solution)/shard_map/reshape | solution.py:143
  309.0 6.7 %all-to-all-start.1 = ((bf16[128,4,2048]{2,1,0:T(4,128)(2,1)}), bf16[128,4,2048]{2,1,0:T(4,128)(2,1)S(1)}, u32[]{:S(2)}, u32[]{:S(2)}) async-start(bf16[128,4,2048]{2,1,0:T(4,128)(2,1)} %reshape.139), calls=%async_computation.1 | async-start | bytes 4194304 | tf_op jit(solution)/shard_map/all_to_all | solution.py:140
  315.7 0.3 all-reduce.5.cloned.1.call-start
  316.1 0.1 mul.147
  316.2 0.2 fusion.39
  316.4 49.3 %all-to-all-done.1 = bf16[128,4,2048]{2,1,0:T(4,128)(2,1)S(1)} async-done(((bf16[128,4,2048]{2,1,0:T(4,128)(2,1)}), bf16[128,4,2048]{2,1,0:T(4,128)(2,1)S(1)}, u32[]{:S(2)}, u32[]{:S(2)}) %all-to-all-start.1) | async-done | bytes 2097184 | tf_op jit(solution)/shard_map/all_to_all | solution.py:140
  365.7 2.7 convert_reduce_fusion
  368.4 2.0 reshape.140
  370.4 1.8 fusion.81
  372.2 26.6 %all-reduce.5.cloned.1.call-done = f32[16,2048]{1,0:T(8,128)} async-done(((f32[16,2048]{1,0:T(8,128)}), f32[16,2048]{1,0:T(8,128)}) %all-reduce.5.cloned.1.call-update) | async-done | bytes 131088 | tf_op jit(solution)/shard_map/psum | solution.py:153
  398.8 1.5 fusion.38
  (52 shorter events, 0.6 us)
Async XLA Ops:
  6.5 293.3 %copy-start = (bf16[1,256,2048]{2,1,0:T(8,128)(2,1)S(1)}, bf16[1,256,2048]{2,1,0:T(8,128)(2,1)}, u32[]{:S(2)}) copy-start(bf16[1,256,2048]{2,1,0:T(8,128)(2,1)} %param.25) | copy-start | bytes 3145732
  6.5 10.6 %copy-start.2 = (bf16[128,2048]{1,0:T(8,128)(2,1)S(1)}, bf16[128,2048]{1,0:T(8,128)(2,1)}, u32[]{:S(2)}) copy-start(bf16[128,2048]{1,0:T(8,128)(2,1)} %param.13) | copy-start | bytes 1572868
  6.5 10.6 %copy-start.8 = (f32[2048]{0:T(1024)S(1)}, f32[2048]{0:T(1024)}, u32[]{:S(2)}) copy-start(f32[2048]{0:T(1024)} %param.15) | copy-start | bytes 24580
  6.5 10.6 %copy-start.7 = (bf16[2048,128]{1,0:T(8,128)(2,1)S(1)}, bf16[2048,128]{1,0:T(8,128)(2,1)}, u32[]{:S(2)}) copy-start(bf16[2048,128]{1,0:T(8,128)(2,1)} %param.16) | copy-start | bytes 1572868
  6.5 221.3 %all-reduce.3.cloned.1.call-start = ((), (), s32[]{:S(2)}) async-start(), calls=%async_computation.2 | async-start | bytes 2097152 | tf_op jit(solution)/shard_map/psum | solution.py:105
  8.0 30.8 %copy-start.4 = (s32[128]{0:T(128)S(1)}, s32[128]{0:T(128)}, u32[]{:S(2)}) copy-start(s32[128]{0:T(128)} %param.14) | copy-start | bytes 1540
  9.6 8.2 %collective-permute-start = (bf16[128,128]{1,0:T(8,128)(2,1)S(1)}, bf16[128,128]{1,0:T(8,128)(2,1)S(1)}, u32[]{:S(2)}, u32[]{:S(2)}) collective-permute-start(bf16[128,128]{1,0:T(8,128)(2,1)S(1)} %convolution_convert_fusion.2), channel_id=1, source_target_pairs={{0,8},{8,16},{16,24},{24,32},{32,40},{40,48},{48,56},{56,64},{64,7... | collective-permute-start | bytes 98312 | tf_op jit(solution)/shard_map/ppermute | solution.py:76
  11.8 42.9 %collective-permute-start.8 = (bf16[128,128]{1,0:T(8,128)(2,1)S(1)}, bf16[128,128]{1,0:T(8,128)(2,1)S(1)}, u32[]{:S(2)}, u32[]{:S(2)}) collective-permute-start(bf16[128,128]{1,0:T(8,128)(2,1)S(1)} %convolution_convert_fusion.2), channel_id=1, source_target_pairs={{8,0},{16,8},{24,16},{32,24},{40,32},{48,40},{56,48},{64,56},{72,6... | collective-permute-start | bytes 98312 | tf_op jit(solution)/shard_map/ppermute | solution.py:78
  17.6 63.0 %copy-start.5 = (s32[16,8]{0,1:T(8,128)S(1)}, s32[16,8]{0,1:T(8,128)}, u32[]{:S(2)}) copy-start(s32[16,8]{0,1:T(8,128)} %param.21) | copy-start | bytes 1540
  17.8 19.7 %collective-permute-start.1 = (bf16[128,128]{1,0:T(8,128)(2,1)S(1)}, bf16[128,128]{1,0:T(8,128)(2,1)S(1)}, u32[]{:S(2)}, u32[]{:S(2)}) collective-permute-start(bf16[128,128]{1,0:T(8,128)(2,1)S(1)} %collective-permute-done), channel_id=1, source_target_pairs={{0,8},{8,16},{16,24},{24,32},{32,40},{40,48},{48,56},{56,64},{64,7... | collective-permute-start | bytes 98312 | tf_op jit(solution)/shard_map/ppermute | solution.py:76
  37.5 18.7 %collective-permute-start.2 = (bf16[128,128]{1,0:T(8,128)(2,1)S(1)}, bf16[128,128]{1,0:T(8,128)(2,1)S(1)}, u32[]{:S(2)}, u32[]{:S(2)}) collective-permute-start(bf16[128,128]{1,0:T(8,128)(2,1)S(1)} %collective-permute-done.1), channel_id=1, source_target_pairs={{0,8},{8,16},{16,24},{24,32},{32,40},{40,48},{48,56},{56,64},{64,7... | collective-permute-start | bytes 98312 | tf_op jit(solution)/shard_map/ppermute | solution.py:76
  54.7 3.1 collective-permute-start.9
  56.2 6.1 %collective-permute-start.3 = (bf16[128,128]{1,0:T(8,128)(2,1)S(1)}, bf16[128,128]{1,0:T(8,128)(2,1)S(1)}, u32[]{:S(2)}, u32[]{:S(2)}) collective-permute-start(bf16[128,128]{1,0:T(8,128)(2,1)S(1)} %collective-permute-done.2), channel_id=1, source_target_pairs={{0,8},{8,16},{16,24},{24,32},{32,40},{40,48},{48,56},{56,64},{64,7... | collective-permute-start | bytes 98312 | tf_op jit(solution)/shard_map/ppermute | solution.py:76
  57.8 5.5 %collective-permute-start.10 = (bf16[128,128]{1,0:T(8,128)(2,1)S(1)}, bf16[128,128]{1,0:T(8,128)(2,1)S(1)}, u32[]{:S(2)}, u32[]{:S(2)}) collective-permute-start(bf16[128,128]{1,0:T(8,128)(2,1)S(1)} %collective-permute-done.9), channel_id=1, source_target_pairs={{8,0},{16,8},{24,16},{32,24},{40,32},{48,40},{56,48},{64,56},{72,6... | collective-permute-start | bytes 98312 | tf_op jit(solution)/shard_map/ppermute | solution.py:78
  62.3 6.1 %collective-permute-start.4 = (bf16[128,128]{1,0:T(8,128)(2,1)S(1)}, bf16[128,128]{1,0:T(8,128)(2,1)S(1)}, u32[]{:S(2)}, u32[]{:S(2)}) collective-permute-start(bf16[128,128]{1,0:T(8,128)(2,1)S(1)} %collective-permute-done.3), channel_id=1, source_target_pairs={{0,8},{8,16},{16,24},{24,32},{32,40},{40,48},{48,56},{56,64},{64,7... | collective-permute-start | bytes 98312 | tf_op jit(solution)/shard_map/ppermute | solution.py:76
  63.3 6.1 %collective-permute-start.11 = (bf16[128,128]{1,0:T(8,128)(2,1)S(1)}, bf16[128,128]{1,0:T(8,128)(2,1)S(1)}, u32[]{:S(2)}, u32[]{:S(2)}) collective-permute-start(bf16[128,128]{1,0:T(8,128)(2,1)S(1)} %collective-permute-done.10), channel_id=1, source_target_pairs={{8,0},{16,8},{24,16},{32,24},{40,32},{48,40},{56,48},{64,56},{72,6... | collective-permute-start | bytes 98312 | tf_op jit(solution)/shard_map/ppermute | solution.py:78
  68.3 6.1 %collective-permute-start.5 = (bf16[128,128]{1,0:T(8,128)(2,1)S(1)}, bf16[128,128]{1,0:T(8,128)(2,1)S(1)}, u32[]{:S(2)}, u32[]{:S(2)}) collective-permute-start(bf16[128,128]{1,0:T(8,128)(2,1)S(1)} %collective-permute-done.4), channel_id=1, source_target_pairs={{0,8},{8,16},{16,24},{24,32},{32,40},{40,48},{48,56},{56,64},{64,7... | collective-permute-start | bytes 98312 | tf_op jit(solution)/shard_map/ppermute | solution.py:76
  69.4 6.1 %collective-permute-start.12 = (bf16[128,128]{1,0:T(8,128)(2,1)S(1)}, bf16[128,128]{1,0:T(8,128)(2,1)S(1)}, u32[]{:S(2)}, u32[]{:S(2)}) collective-permute-start(bf16[128,128]{1,0:T(8,128)(2,1)S(1)} %collective-permute-done.11), channel_id=1, source_target_pairs={{8,0},{16,8},{24,16},{32,24},{40,32},{48,40},{56,48},{64,56},{72,6... | collective-permute-start | bytes 98312 | tf_op jit(solution)/shard_map/ppermute | solution.py:78
  74.4 6.1 %collective-permute-start.6 = (bf16[128,128]{1,0:T(8,128)(2,1)S(1)}, bf16[128,128]{1,0:T(8,128)(2,1)S(1)}, u32[]{:S(2)}, u32[]{:S(2)}) collective-permute-start(bf16[128,128]{1,0:T(8,128)(2,1)S(1)} %collective-permute-done.5), channel_id=1, source_target_pairs={{0,8},{8,16},{16,24},{24,32},{32,40},{40,48},{48,56},{56,64},{64,7... | collective-permute-start | bytes 98312 | tf_op jit(solution)/shard_map/ppermute | solution.py:76
  75.4 6.1 %collective-permute-start.13 = (bf16[128,128]{1,0:T(8,128)(2,1)S(1)}, bf16[128,128]{1,0:T(8,128)(2,1)S(1)}, u32[]{:S(2)}, u32[]{:S(2)}) collective-permute-start(bf16[128,128]{1,0:T(8,128)(2,1)S(1)} %collective-permute-done.12), channel_id=1, source_target_pairs={{8,0},{16,8},{24,16},{32,24},{40,32},{48,40},{56,48},{64,56},{72,6... | collective-permute-start | bytes 98312 | tf_op jit(solution)/shard_map/ppermute | solution.py:78
  80.5 6.1 %collective-permute-start.7 = (bf16[128,128]{1,0:T(8,128)(2,1)S(1)}, bf16[128,128]{1,0:T(8,128)(2,1)S(1)}, u32[]{:S(2)}, u32[]{:S(2)}) collective-permute-start(bf16[128,128]{1,0:T(8,128)(2,1)S(1)} %collective-permute-done.6), channel_id=1, source_target_pairs={{0,8},{8,16},{16,24},{24,32},{32,40},{40,48},{48,56},{56,64},{64,7... | collective-permute-start | bytes 98312 | tf_op jit(solution)/shard_map/ppermute | solution.py:76
  81.5 14.3 %collective-permute-start.14 = (bf16[128,128]{1,0:T(8,128)(2,1)S(1)}, bf16[128,128]{1,0:T(8,128)(2,1)S(1)}, u32[]{:S(2)}, u32[]{:S(2)}) collective-permute-start(bf16[128,128]{1,0:T(8,128)(2,1)S(1)} %collective-permute-done.13), channel_id=1, source_target_pairs={{8,0},{16,8},{24,16},{32,24},{40,32},{48,40},{56,48},{64,56},{72,6... | collective-permute-start | bytes 98312 | tf_op jit(solution)/shard_map/ppermute | solution.py:78
  98.1 130.8 %copy-start.3 = (f32[2048]{0:T(1024)S(1)}, f32[2048]{0:T(1024)}, u32[]{:S(2)}) copy-start(f32[2048]{0:T(1024)} %param.20) | copy-start | bytes 24580
  296.3 3.5 copy-start.1
  309.0 7.0 %copy-start.6 = (f32[16,8]{0,1:T(8,128)S(1)}, f32[16,8]{0,1:T(8,128)}, u32[]{:S(2)}) copy-start(f32[16,8]{0,1:T(8,128)} %param.22) | copy-start | bytes 1540
  309.0 56.7 %all-to-all-start.1 = ((bf16[128,4,2048]{2,1,0:T(4,128)(2,1)}), bf16[128,4,2048]{2,1,0:T(4,128)(2,1)S(1)}, u32[]{:S(2)}, u32[]{:S(2)}) async-start(bf16[128,4,2048]{2,1,0:T(4,128)(2,1)} %reshape.139), calls=%async_computation.1 | async-start | bytes 4194304 | tf_op jit(solution)/shard_map/all_to_all | solution.py:140
  315.7 83.0 %all-reduce.5.cloned.1.call-start = ((), (), s32[]{:S(2)}) async-start(), calls=%async_computation.3 | async-start | bytes 262144 | tf_op jit(solution)/shard_map/psum | solution.py:153
Sparse Core Ops, SparseCore 0:
  101.0 126.7 all-reduce.2
  372.3 26.4 all-reduce.4
